TPU v7x, 32 devices: a whole 2x2x4 slice. The times are simulated.
32 devices in a mesh: dp: 4 (over z), expert: 8 (over y, x, core).
Axes of the slice: x: 2, y: 2, z: 4, core: 2. Of those that a mesh axis runs over, the one named last changes fastest.
Arguments:
- hidden: bfloat16 [3072, 2880], P('expert', 'dp'), may hold values from -6 to 6
- segments: int32 [8, 384], P('expert'), may hold values from 0 to 3, never falling along the last dimension, each value on 1 to 192 neighbouring positions
- request_adapter: int32 [8, 4], P('expert'), may hold values from 0 to 7
- routes: int32 [8, 384, 4], P('expert', 'dp'), may hold values from 0 to 7, all different within a row; in each aligned block of 96 rows (0 to 95, 96 to 191, ..., all dimensions but the last counted through in order) at most 64 rows name the same one
- expert_gates: bfloat16 [8, 384, 4], P('expert', 'dp'), may hold values from 0.049804688 to 0.59765625
- attention_gain: float32 [2880], replicated, may hold values from 0.25 to 1.75
- joined_weight: bfloat16 [2880, 4, 640], P(None, 'dp'), may hold values from -0.109375 to 0.109375
- sinks: float32 [32], P('dp'), may hold values from 0 to 3
- attention_out_weight: bfloat16 [2048, 2880], P('dp'), may hold values from -0.125 to 0.125
- joined_down_maps: bfloat16 [2880, 128], replicated, may hold values from -0.109375 to 0.109375
- joined_up_maps: bfloat16 [128, 4, 640], P(None, 'dp'), may hold values from -0.375 to 0.375
- output_down_maps: bfloat16 [2048, 128], P('dp'), may hold values from -0.125 to 0.125
- output_up_maps: bfloat16 [128, 2880], P(None, 'dp'), may hold values from -0.75 to 0.75
- expert_norm_gain: float32 [2880], replicated, may hold values from 0.25 to 1.75
- expert_gate_weight: bfloat16 [8, 2880, 2880], P('expert', None, 'dp'), may hold values from -0.109375 to 0.109375
- expert_up_weight: bfloat16 [8, 2880, 2880], P('expert', None, 'dp'), may hold values from -0.109375 to 0.109375
- expert_down_weight: bfloat16 [8, 2880, 2880], P('expert', 'dp'), may hold values from -0.109375 to 0.109375
- closing_gain: float32 [2880], replicated, may hold values from 0.25 to 1.75
- vocabulary_weight: bfloat16 [2880, 25600], P(None, ('dp', 'expert')), may hold values from -0.109375 to 0.109375
Outputs:
- hidden_out: bfloat16 [3072, 2880], P('expert', 'dp')
- logits: float32 [32, 25600], P(None, ('dp', 'expert'))
Inputs may be any that keep to these rules, and one draw needn't show every extreme that they name: `segments`: in each column the ids do not fall; each of the 4 requests has 1 to 192 tokens, and one has exactly 192. `routes`: the 4 experts of a token differ. Within the rows of one device (96 consecutive tokens, aligned blocks) no expert is named more than 64 times, and in some blocks one expert is named exactly 64 times.
All inputs are finite; a program needn't handle non-finite values.
Results may differ from a plain program's by a relative error of at most 0.02.
Values may be sent and summed in bfloat16 or wider, within the bound.
No kernel may reach another device: no remote copies, remote signals or barrier semaphores. Data moves between devices by JAX's collectives and lax.ppermute only.
A program may use at most 128 MiB of HBM per device.

v0:
```python
import jax
import jax.numpy as jnp
from jax import lax
from jax.sharding import PartitionSpec as P

HEAD_SIZE = 64
QUERY_GROUP = 8
TOP = 4
ADAPTER_RANK = 16
REQS = 4
epsilon = 1e-05
theta_base = 150000.0
adapter_scale = 2.0
glu_alpha = 1.702


def rms_scale(values, gain_row):
    mean_square = jnp.mean(values * values, axis=-1, keepdims=True)
    return values * lax.rsqrt(mean_square + epsilon) * gain_row


def positions_of(segment_row):
    counter = jnp.arange(segment_row.shape[0], dtype=jnp.int32)
    starting = jnp.concatenate(
        [jnp.ones((1,), dtype=jnp.bool_), segment_row[1:] != segment_row[:-1]]
    )
    first_index = lax.cummax(jnp.where(starting, counter, 0), axis=0)
    return counter - first_index


def adapter_per_token(segment_row, adapter_row):
    hits = segment_row[:, None] == jnp.arange(adapter_row.shape[0], dtype=jnp.int32)[None, :]
    return jnp.sum(jnp.where(hits, adapter_row[None, :], 0), axis=1)


def rotate_heads(values, positions):
    head_dim = values.shape[-1]
    half_dim = head_dim // 2
    frequency = theta_base ** (-2.0 * jnp.arange(half_dim, dtype=jnp.float32) / head_dim)
    angles = positions.astype(jnp.float32)[:, None] * frequency[None, :]
    cosine = jnp.cos(angles)[:, None, :]
    sine_part = jnp.sin(angles)[:, None, :]
    first_half = values[..., :half_dim]
    second_half = values[..., half_dim:]
    return jnp.concatenate(
        [
            first_half * cosine - second_half * sine_part,
            second_half * cosine + first_half * sine_part,
        ],
        axis=-1,
    )


def attend_heads(queries, key_heads, value_heads, segment_row, sink_row):
    tokens_now, kv_now, group_now, head_dim = queries.shape
    scores = jnp.einsum(
        "tkgh,skh->kgts", queries, key_heads, preferred_element_type=jnp.float32
    ) * head_dim ** (-0.5)
    counter = jnp.arange(tokens_now, dtype=jnp.int32)
    allowed = (segment_row[:, None] == segment_row[None, :]) & (
        counter[None, :] <= counter[:, None]
    )
    weights = jnp.where(allowed[None, None], jnp.exp(scores), 0.0)
    totals = jnp.sum(weights, axis=-1, keepdims=True) + jnp.exp(sink_row).reshape(
        kv_now, group_now, 1, 1
    )
    probs = (weights / totals).astype(jnp.bfloat16)
    blended_hidden = jnp.einsum(
        "kgts,skh->tkgh", probs, value_heads, preferred_element_type=jnp.float32
    )
    return blended_hidden.astype(jnp.bfloat16).reshape(tokens_now, kv_now * group_now * head_dim)


def shards(
    hidden,
    segments,
    request_adapter,
    routes,
    expert_gates,
    attention_gain,
    joined_weight,
    sinks,
    attention_out_weight,
    joined_down_maps,
    joined_up_maps,
    output_down_maps,
    output_up_maps,
    expert_norm_gain,
    expert_gate_weight,
    expert_up_weight,
    expert_down_weight,
    closing_gain,
    vocabulary_weight,
):
    groups = lax.axis_size("dp")
    columns = lax.axis_size("expert")
    position_dp = lax.axis_index("dp")
    segment_row = segments[0]
    adapter_row = request_adapter[0]
    col_tokens = segment_row.shape[0]
    gathered_rows = lax.all_gather(hidden, "dp", axis=1, tiled=True)
    width = gathered_rows.shape[1]
    normalized_hidden = rms_scale(gathered_rows.astype(jnp.float32), attention_gain).astype(
        jnp.bfloat16
    )
    joined_projection = jnp.dot(
        normalized_hidden, joined_weight.reshape(width, -1), preferred_element_type=jnp.float32
    )
    reduced_every_adapter = joined_down_maps.shape[1]
    reduced_hidden = jnp.dot(
        normalized_hidden, joined_down_maps, preferred_element_type=jnp.float32
    ).astype(jnp.bfloat16)
    rank_owner = jnp.arange(reduced_every_adapter, dtype=jnp.int32) // ADAPTER_RANK
    adapter_mask = adapter_per_token(segment_row, adapter_row)[:, None] == rank_owner[None, :]
    selected_reduced = jnp.where(adapter_mask, reduced_hidden, jnp.zeros_like(reduced_hidden))
    joined_projection = joined_projection + adapter_scale * jnp.dot(
        selected_reduced,
        joined_up_maps.reshape(reduced_every_adapter, -1),
        preferred_element_type=jnp.float32,
    )
    kv_here = joined_weight.shape[1]
    joined_projection = joined_projection.reshape(col_tokens, kv_here, QUERY_GROUP + 2, HEAD_SIZE)
    positions = positions_of(segment_row)
    queries = rotate_heads(
        joined_projection[:, :, :QUERY_GROUP].reshape(col_tokens, kv_here * QUERY_GROUP, HEAD_SIZE),
        positions,
    )
    queries = queries.astype(jnp.bfloat16).reshape(col_tokens, kv_here, QUERY_GROUP, HEAD_SIZE)
    key_heads = rotate_heads(joined_projection[:, :, QUERY_GROUP], positions).astype(jnp.bfloat16)
    value_heads = joined_projection[:, :, QUERY_GROUP + 1].astype(jnp.bfloat16)
    blended_hidden = attend_heads(queries, key_heads, value_heads, segment_row, sinks)
    share = col_tokens // groups
    quarter = hidden.shape[1]
    rank_total = output_down_maps.shape[1]
    route_pack = jnp.concatenate(
        [routes[0].astype(jnp.bfloat16), expert_gates[0].astype(jnp.bfloat16)], axis=1
    )
    pack_width = -(quarter + rank_total) % 128 or 128
    route_pack = jnp.pad(route_pack, ((0, 0), (0, pack_width - 2 * TOP)))
    pack_rows = lax.dynamic_update_slice_in_dim(
        jnp.zeros((col_tokens, pack_width), jnp.bfloat16), route_pack, position_dp * share, 0
    )
    partial_out = jnp.dot(blended_hidden, attention_out_weight, preferred_element_type=jnp.float32)
    low_local = jnp.dot(blended_hidden, output_down_maps, preferred_element_type=jnp.float32)
    joined_send = jnp.concatenate(
        [
            partial_out.astype(jnp.bfloat16).reshape(col_tokens, groups, quarter),
            jnp.broadcast_to(
                low_local.astype(jnp.bfloat16)[:, None, :], (col_tokens, groups, rank_total)
            ),
            jnp.broadcast_to(pack_rows[:, None, :], (col_tokens, groups, pack_width)),
        ],
        axis=2,
    ).reshape(col_tokens, -1)
    reduced_parts = []

    def reduce_rows(lo, rows):
        joined_back = lax.psum_scatter(
            joined_send[lo : lo + rows], "dp", scatter_dimension=1, tiled=True
        )
        return joined_back

    def resid_rows(joined_back, lo, rows):
        mine_out = joined_back[:, :quarter].astype(jnp.float32)
        output_reduced = joined_back[:, quarter : quarter + rank_total]
        selected_output = jnp.where(
            adapter_mask[lo : lo + rows], output_reduced, jnp.zeros_like(output_reduced)
        )
        adapter_delta = adapter_scale * jnp.dot(
            selected_output, output_up_maps, preferred_element_type=jnp.float32
        )
        resid_part = (hidden[lo : lo + rows].astype(jnp.float32) + mine_out + adapter_delta).astype(
            jnp.bfloat16
        )
        return (resid_part, joined_back[:, quarter + rank_total :])

    lane_pad = -width % 128
    wide = width + lane_pad
    experts = expert_gate_weight.shape[0] * columns
    capacity = 4 * share * TOP // (3 * experts)
    gate_weight = expert_gate_weight[0]
    up_weight = expert_up_weight[0]
    down_weight = jnp.pad(expert_down_weight[0], ((0, 0), (0, lane_pad)))
    halves = 2 if groups % 2 == 0 else 1
    half_tokens = col_tokens // halves
    half_capacity = groups // halves * capacity
    counter = jnp.arange(col_tokens, dtype=jnp.int32)
    request_ids = jnp.arange(REQS, dtype=jnp.int32)
    last_index = jnp.max(
        jnp.where(segment_row[None, :] == request_ids[:, None], counter[None, :], -1), axis=1
    )
    last_index = jnp.clip(last_index, 0, col_tokens - 1)
    moe_rows = []
    last_parts = []
    last_resid_parts = []
    held = None
    pending = None
    for h in range(halves):
        lo = h * half_tokens
        joined_h = reduce_rows(lo, half_tokens)
        resid_h, pack_h = resid_rows(joined_h, lo, half_tokens)
        reduced_parts.append(resid_h)
        column_h = lax.all_gather(resid_h, "dp", axis=1, tiled=True)
        if held is not None:
            column_h, held = lax.optimization_barrier((column_h, held))
        moe_in = rms_scale(column_h.astype(jnp.float32), expert_norm_gain).astype(jnp.bfloat16)
        moe_in = jnp.pad(moe_in, ((0, 0), (0, lane_pad)))
        route_flat = pack_h[:, :TOP].astype(jnp.int32).reshape(-1)
        gates_h = pack_h[:, TOP : 2 * TOP]
        one_hot = (route_flat[:, None] == jnp.arange(experts, dtype=jnp.int32)[None, :]).astype(
            jnp.int32
        )
        slot_rows = jnp.sum((jnp.cumsum(one_hot, axis=0) - one_hot) * one_hot, axis=1)
        target = route_flat * half_capacity + slot_rows
        source_rows = jnp.arange(route_flat.shape[0], dtype=jnp.int32) // TOP
        table = (
            jnp.full((experts * half_capacity,), half_tokens, jnp.int32).at[target].set(source_rows)
        )
        dispatch = (table[:, None] == jnp.arange(half_tokens, dtype=jnp.int32)[None, :]).astype(
            jnp.bfloat16
        )
        outgoing = (
            jnp.dot(dispatch, moe_in, preferred_element_type=jnp.float32)
            .astype(jnp.bfloat16)
            .reshape(experts, half_capacity, wide)
        )
        arrived = lax.all_to_all(outgoing, "expert", split_axis=0, concat_axis=0, tiled=True)
        if h == 0:
            held = arrived
        else:
            arrived = lax.optimization_barrier((arrived, held))[0]
        rows_in = arrived.reshape(-1, wide)[:, :width]
        gate_part = jnp.dot(rows_in, gate_weight, preferred_element_type=jnp.float32)
        up_part = jnp.dot(rows_in, up_weight, preferred_element_type=jnp.float32)
        activated = (gate_part * jax.nn.sigmoid(glu_alpha * gate_part) * (up_part + 1.0)).astype(
            jnp.bfloat16
        )
        shares_out = (
            jnp.dot(activated, down_weight, preferred_element_type=jnp.float32)
            .astype(jnp.bfloat16)
            .reshape(experts, half_capacity, wide)
        )
        answers = lax.all_to_all(shares_out, "expert", split_axis=0, concat_axis=0, tiled=True)
        if pending is not None:
            moe_rows.append(lax.psum_scatter(pending, "dp", scatter_dimension=1, tiled=True))
            answers, moe_rows[-1] = lax.optimization_barrier((answers, moe_rows[-1]))
            pending = None
        slot_ids = jnp.arange(experts * half_capacity, dtype=jnp.int32)
        combine = jnp.sum(
            jnp.where(
                target.reshape(half_tokens, TOP)[:, :, None] == slot_ids[None, None, :],
                gates_h[:, :, None],
                jnp.zeros((), jnp.bfloat16),
            ),
            axis=1,
        ).astype(jnp.bfloat16)
        mixture = jnp.dot(
            combine,
            answers.reshape(experts * half_capacity, wide),
            preferred_element_type=jnp.float32,
        )[:, :width]
        local_last = jnp.clip(last_index - lo, 0, half_tokens - 1)
        inside = ((last_index >= lo) & (last_index < lo + half_tokens))[:, None]
        last_parts.append(
            jnp.where(inside, jnp.take(mixture, local_last, axis=0), jnp.zeros((), jnp.float32))
        )
        last_resid_parts.append(
            jnp.where(inside, jnp.take(column_h, local_last, axis=0), jnp.zeros((), jnp.bfloat16))
        )
        if h < halves - 1:
            pending = mixture.astype(jnp.bfloat16)
        else:
            last_mix = sum(last_parts).reshape(REQS * groups, quarter)
            moe_send = jnp.concatenate([mixture, jnp.tile(last_mix, (1, groups))], axis=0).astype(
                jnp.bfloat16
            )
            moe_rows.append(lax.psum_scatter(moe_send, "dp", scatter_dimension=1, tiled=True))
    moe_back = jnp.concatenate(moe_rows, axis=0)
    moe_rounded = moe_back[:col_tokens].astype(jnp.float32).astype(jnp.bfloat16)
    resid = jnp.concatenate(reduced_parts, axis=0)
    hidden_out = (resid.astype(jnp.float32) + moe_rounded.astype(jnp.float32)).astype(jnp.bfloat16)
    last_moe = moe_back[col_tokens:].reshape(REQS, width)
    last_resid = sum((part.astype(jnp.float32) for part in last_resid_parts))
    last_hidden = (last_resid + last_moe.astype(jnp.float32)).astype(jnp.bfloat16)
    ends = rms_scale(last_hidden.astype(jnp.float32), closing_gain).astype(jnp.bfloat16)
    tail_rows = lax.all_gather(ends, "expert", axis=0, tiled=True)
    logits = jnp.dot(tail_rows, vocabulary_weight, preferred_element_type=jnp.float32)
    return (hidden_out, logits)


def solution(mesh):
    in_specs = (
        P("expert", "dp"),
        P("expert", None),
        P("expert", None),
        P("expert", "dp", None),
        P("expert", "dp", None),
        P(),
        P(None, "dp", None),
        P("dp"),
        P("dp", None),
        P(),
        P(None, "dp", None),
        P("dp", None),
        P(None, "dp"),
        P(),
        P("expert", None, "dp"),
        P("expert", None, "dp"),
        P("expert", "dp", None),
        P(),
        P(None, ("dp", "expert")),
    )
    out_specs = (P("expert", "dp"), P(None, ("dp", "expert")))
    return jax.shard_map(shards, mesh=mesh, in_specs=in_specs, out_specs=out_specs, check_vma=False)
```

profile of v0, /device:TPU:0, one launch (start us, length us, event | category | flops | bytes accessed | tf_op | source)
XLA Modules:
  0.0 549.6 jit_solution(267624168265766925)
XLA Ops:
  13.7 46.6 %all-gather.7.cloned.1.call-done = bf16[384,2880]{0,1:T(8,128)(2,1)} async-done(((bf16[384,720]{0,1:T(8,128)(2,1)}), bf16[384,2880]{0,1:T(8,128)(2,1)}) %all-gather.7.cloned.1.call-update) | async-done | bytes 2211856 | tf_op jit(solution)/shard_map/all_gather | solution.py:101
  60.4 2.2 fusion.12
  62.6 5.9 %fusion.22 = f32[384,640]{1,0:T(8,128)} fusion(bf16[2880,1,640]{2,0,1:T(8,128)(2,1)} %param.29, bf16[384,2880]{0,1:T(8,128)(2,1)} %all-gather.7.cloned.1.call-done, f32[2880]{0:T(1024)S(1)} %copy-done.16, f32[384]{0:T(512)S(1)} %add_rsqrt_fusion), kind=kOutput, calls=%fused_computation.37 | convolution fusion | flops 1420001280 | bytes 6894336 | tf_op jit(solution)/shard_map/dot_general | solution.py:106
  68.5 4.8 fusion.56
  73.3 2.5 copy.64
  76.7 1.2 slice_bitcast_fusion
  78.3 1.3 fusion.19
  79.6 2.2 fusion.59
  82.4 1.7 convolution_convert_fusion.4
  84.4 2.9 fusion.136
  88.4 37.4 %reduce-scatter.13.cloned.1.call-done = bf16[896,192]{1,0:T(8,128)(2,1)} async-done(((bf16[3584,192]{1,0:T(8,128)(2,1)}), bf16[896,192]{1,0:T(8,128)(2,1)}) %reduce-scatter.13.cloned.1.call-update) | async-done | bytes 344080
  130.1 1.7 reduce-window.29
  132.7 3.4 scatter_custom_fusion.1
  136.1 22.6 %all-gather.11.cloned.1.call-done = bf16[4,720,192]{1,2,0:T(8,128)(2,1)} async-done(((bf16[1,720,192]{1,2,0:T(8,128)(2,1)}), bf16[4,720,192]{1,2,0:T(8,128)(2,1)}) %all-gather.11.cloned.1.call-update) | async-done | bytes 1105936 | tf_op jit(solution)/shard_map/all_gather | solution.py:203
  158.6 2.2 copy.75
  162.5 4.5 convolution_convert_fusion.1
  166.9 4.7 all-to-all-start
  172.5 41.0 %reduce-scatter.15.cloned.1.call-done = bf16[896,192]{1,0:T(8,128)(2,1)} async-done(((bf16[3584,192]{1,0:T(8,128)(2,1)}), bf16[896,192]{1,0:T(8,128)(2,1)}) %reduce-scatter.15.cloned.1.call-update) | async-done | bytes 344080
  217.8 1.7 reduce-window.25
  220.4 3.6 scatter_custom_fusion
  223.9 22.4 %all-gather.9.cloned.1.call-done = bf16[4,720,192]{1,2,0:T(8,128)(2,1)} async-done(((bf16[1,720,192]{1,2,0:T(8,128)(2,1)}), bf16[4,720,192]{1,2,0:T(8,128)(2,1)}) %all-gather.9.cloned.1.call-update) | async-done | bytes 1105936 | tf_op jit(solution)/shard_map/all_gather | solution.py:203
  246.4 3.2 copy.72
  249.6 2.7 reshape.552
  253.0 4.4 convolution_convert_fusion
  257.4 4.7 all-to-all-start.1
  262.1 10.4 %fusion.4 = f32[1024,720]{0,1:T(8,128)} fusion(bf16[1024,2944]{1,0:T(8,128)(2,1)} %bitcast.45, bf16[1,2880,720]{1,2,0:T(8,128)(2,1)} %param.38), kind=kOutput, calls=%fused_computation.16 | convolution fusion | flops 4246732800 | bytes 13125632 | tf_op jit(solution)/shard_map/dot_general | solution.py:234
  272.5 16.8 %convolution_convert_fusion.2 = bf16[1024,2944]{1,0:T(8,128)(2,1)} fusion(bf16[720,2880]{1,0:T(8,128)(2,1)} %bitcast.183, f32[1024,720]{0,1:T(8,128)} %fusion.4, bf16[1,2880,720]{1,2,0:T(8,128)(2,1)} %param.37, bf16[1024,2944]{1,0:T(8,128)(2,1)} %bitcast.45), kind=kOutput, calls=%fused_computation.12 | convolution fusion | flops 8596750336 | bytes 23302144 | tf_op jit(solution)/shard_map/dot_general | solution.py:239
  289.3 41.6 %all-to-all-done.1 = bf16[8,128,2944]{2,1,0:T(8,128)(2,1)} async-done(((bf16[8,128,2944]{2,1,0:T(8,128)(2,1)}), bf16[8,128,2944]{2,1,0:T(8,128)(2,1)}, u32[]{:S(2)}, u32[]{:S(2)}) %all-to-all-start.1) | async-done | bytes 6029344 | tf_op jit(solution)/shard_map/all_to_all | solution.py:227
  330.9 4.9 all-to-all-start.3
  335.8 10.4 %fusion.8 = f32[1024,720]{0,1:T(8,128)} fusion(bf16[1024,2944]{1,0:T(8,128)(2,1)} %bitcast.40, bf16[1,2880,720]{1,2,0:T(8,128)(2,1)} %param.38), kind=kOutput, calls=%fused_computation.20 | convolution fusion | flops 4246732800 | bytes 13125632 | tf_op jit(solution)/shard_map/dot_general | solution.py:234
  346.2 16.8 %convolution_convert_fusion.3 = bf16[1024,2944]{1,0:T(8,128)(2,1)} fusion(bf16[720,2880]{1,0:T(8,128)(2,1)} %bitcast.184, f32[1024,720]{0,1:T(8,128)} %fusion.8, bf16[1,2880,720]{1,2,0:T(8,128)(2,1)} %param.37, bf16[1024,2944]{1,0:T(8,128)(2,1)} %bitcast.40), kind=kOutput, calls=%fused_computation.13 | convolution fusion | flops 8596750336 | bytes 23302144 | tf_op jit(solution)/shard_map/dot_general | solution.py:239
  363.0 41.6 %all-to-all-done.3 = bf16[8,128,2944]{2,1,0:T(8,128)(2,1)} async-done(((bf16[8,128,2944]{2,1,0:T(8,128)(2,1)}), bf16[8,128,2944]{2,1,0:T(8,128)(2,1)}, u32[]{:S(2)}, u32[]{:S(2)}) %all-to-all-start.3) | async-done | bytes 6029344 | tf_op jit(solution)/shard_map/all_to_all | solution.py:243
  404.6 4.7 all-to-all-start.2
  409.9 5.8 %fusion.140 = (bf16[192,2880]{1,0:T(8,128)(2,1)}, f32[192,2880]{1,0:T(8,128)}) fusion(bf16[192,1024]{1,0:T(8,128)(2,1)S(1)} %fusion.51, bf16[1024,2944]{1,0:T(8,128)(2,1)} %bitcast.47), kind=kOutput, calls=%fused_computation.218 | convolution fusion | flops 1133015040 | bytes 9740288 | tf_op jit(solution)/shard_map/dot_general | solution.py:257
  415.7 2.5 copy.88
  419.1 2.2 gather_fusion
  421.3 30.4 %reduce-scatter.17.cloned.1.call-done = bf16[720,192]{1,0:T(8,128)(2,1)} async-done(((bf16[2880,192]{1,0:T(8,128)(2,1)}), bf16[720,192]{1,0:T(8,128)(2,1)}) %reduce-scatter.17.cloned.1.call-update) | async-done | bytes 276496
  451.7 1.8 copy.89
  453.6 24.6 %all-to-all-done.2 = bf16[8,128,2944]{2,1,0:T(8,128)(2,1)} async-done(((bf16[8,128,2944]{2,1,0:T(8,128)(2,1)}), bf16[8,128,2944]{2,1,0:T(8,128)(2,1)}, u32[]{:S(2)}, u32[]{:S(2)}) %all-to-all-start.2) | async-done | bytes 6029344 | tf_op jit(solution)/shard_map/all_to_all | solution.py:243
  478.2 5.8 %fusion.141 = (bf16[192,2880]{1,0:T(8,128)(2,1)}, f32[192,2880]{1,0:T(8,128)}) fusion(bf16[192,1024]{1,0:T(8,128)(2,1)S(1)} %fusion.50, bf16[1024,2944]{1,0:T(8,128)(2,1)} %bitcast.48), kind=kOutput, calls=%fused_computation.219 | convolution fusion | flops 1133015040 | bytes 9740288 | tf_op jit(solution)/shard_map/dot_general | solution.py:257
  484.0 2.2 gather_fusion.1
  486.6 2.4 pad_maximum_fusion.1
  489.0 2.6 copy.90
  491.6 1.2 gather_fusion.2
  492.8 1.2 gather_fusion.3
  494.0 28.9 %reduce-scatter.19.cloned.1.call-done = bf16[720,208]{1,0:T(8,128)(2,1)} async-done(((bf16[2880,208]{1,0:T(8,128)(2,1)}), bf16[720,208]{1,0:T(8,128)(2,1)}) %reduce-scatter.19.cloned.1.call-update) | async-done | bytes 299536
  528.8 9.2 %all-gather.2 = bf16[8,4,2880]{2,1,0:T(4,128)(2,1)S(1)} all-gather(bf16[1,4,2880]{2,1,0:T(4,128)(2,1)S(1)} %fusion.108), channel_id=1, replica_groups=mesh['dp'=4,'expert'=8] {'expert'}, dimensions={0}, use_global_device_ids=true | all-gather | bytes 207360 | tf_op jit(solution)/shard_map/all_gather | solution.py:286
  538.1 4.4 fusion.142
  (149 shorter events, 30.5 us)
Async XLA Ops:
  7.2 75.2 %copy-start = (bf16[512,2880]{0,1:T(8,128)(2,1)S(1)}, bf16[512,2880]{0,1:T(8,128)(2,1)}, u32[]{:S(2)}) copy-start(bf16[512,2880]{0,1:T(8,128)(2,1)} %param.31) | copy-start | bytes 8847364
  7.2 55.4 %copy-start.16 = (f32[2880]{0:T(1024)S(1)}, f32[2880]{0:T(1024)}, u32[]{:S(2)}) copy-start(f32[2880]{0:T(1024)} %param.28) | copy-start | bytes 34564
  7.2 53.2 %all-gather.7.cloned.1.call-start = ((), (), s32[]{:S(2)}) async-start(), calls=%async_computation.8 | async-start | bytes 2764800 | tf_op jit(solution)/shard_map/all_gather | solution.py:101
  7.9 117.9 %reduce-scatter.13.cloned.1.call-start = ((), (), s32[]{:S(2)}) async-start(), calls=%async_computation.11 | async-start | bytes 2293760
  12.4 0.9 copy-start.7
  62.6 5.9 %copy-start.15 = (bf16[128,1,640]{2,0,1:T(8,128)(2,1)S(1)}, bf16[128,1,640]{2,0,1:T(8,128)(2,1)}, u32[]{:S(2)}) copy-start(bf16[128,1,640]{2,0,1:T(8,128)(2,1)} %param.33) | copy-start | bytes 491524
  79.6 2.3 copy-start.9
  82.3 1.7 copy-start.8
  84.4 3.5 copy-start.2
  87.4 40.6 %copy-start.5 = (bf16[128,720]{0,1:T(8,128)(2,1)S(1)}, bf16[128,720]{0,1:T(8,128)(2,1)}, u32[]{:S(2)}) copy-start(bf16[128,720]{0,1:T(8,128)(2,1)} %param.35) | copy-start | bytes 552964
  87.4 71.3 %all-gather.11.cloned.1.call-start = ((), (), s32[]{:S(2)}) async-start(), calls=%async_computation.10 | async-start | bytes 1474560 | tf_op jit(solution)/shard_map/all_gather | solution.py:203
  132.5 29.6 %copy-start.10 = (f32[2880]{0:T(1024)S(1)}, f32[2880]{0:T(1024)}, u32[]{:S(2)}) copy-start(f32[2880]{0:T(1024)} %param.36) | copy-start | bytes 34564
  166.9 85.3 %all-to-all-start = ((bf16[8,128,2944]{2,1,0:T(8,128)(2,1)}), bf16[8,128,2944]{2,1,0:T(8,128)(2,1)}, u32[]{:S(2)}, u32[]{:S(2)}) async-start(bf16[8,128,2944]{2,1,0:T(8,128)(2,1)} %bitcast.149), calls=%async_computation | async-start | bytes 12058624 | tf_op jit(solution)/shard_map/all_to_all | solution.py:227
  171.7 44.0 %copy-start.6 = (bf16[128,720]{0,1:T(8,128)(2,1)S(1)}, bf16[128,720]{0,1:T(8,128)(2,1)}, u32[]{:S(2)}) copy-start(bf16[128,720]{0,1:T(8,128)(2,1)} %param.35) | copy-start | bytes 552964
  171.7 41.8 %reduce-scatter.15.cloned.1.call-start = ((), (), s32[]{:S(2)}) async-start(), calls=%async_computation.12 | async-start | bytes 2293760
  172.3 74.1 %all-gather.9.cloned.1.call-start = ((), (), s32[]{:S(2)}) async-start(), calls=%async_computation.9 | async-start | bytes 1474560 | tf_op jit(solution)/shard_map/all_gather | solution.py:203
  257.4 73.5 %all-to-all-start.1 = ((bf16[8,128,2944]{2,1,0:T(8,128)(2,1)}), bf16[8,128,2944]{2,1,0:T(8,128)(2,1)}, u32[]{:S(2)}, u32[]{:S(2)}) async-start(bf16[8,128,2944]{2,1,0:T(8,128)(2,1)} %bitcast.150), calls=%async_computation.1 | async-start | bytes 12058624 | tf_op jit(solution)/shard_map/all_to_all | solution.py:227
  330.9 73.7 %all-to-all-start.3 = ((bf16[8,128,2944]{2,1,0:T(8,128)(2,1)}), bf16[8,128,2944]{2,1,0:T(8,128)(2,1)}, u32[]{:S(2)}, u32[]{:S(2)}) async-start(bf16[8,128,2944]{2,1,0:T(8,128)(2,1)} %bitcast.158), calls=%async_computation.3 | async-start | bytes 12058624 | tf_op jit(solution)/shard_map/all_to_all | solution.py:243
  404.6 73.5 %all-to-all-start.2 = ((bf16[8,128,2944]{2,1,0:T(8,128)(2,1)}), bf16[8,128,2944]{2,1,0:T(8,128)(2,1)}, u32[]{:S(2)}, u32[]{:S(2)}) async-start(bf16[8,128,2944]{2,1,0:T(8,128)(2,1)} %bitcast.157), calls=%async_computation.2 | async-start | bytes 12058624 | tf_op jit(solution)/shard_map/all_to_all | solution.py:243
  409.4 42.4 %reduce-scatter.17.cloned.1.call-start = ((), (), s32[]{:S(2)}) async-start(), calls=%async_computation.13 | async-start | bytes 1843200
  418.3 104.5 %reduce-scatter.19.cloned.1.call-start = ((), (), s32[]{:S(2)}) async-start(), calls=%async_computation.14 | async-start | bytes 1843200
  418.5 67.7 %copy-start.12 = (pred[4]{0:T(512)(128)(4,1)}, pred[4]{0:T(512)(128)(4,1)S(1)}, u32[]{:S(2)}) copy-start(pred[4]{0:T(512)(128)(4,1)S(1)} %get-tuple-element.42) | copy-start | bytes 16
  418.5 67.7 %copy-start.13 = (pred[4]{0:T(512)(128)(4,1)}, pred[4]{0:T(512)(128)(4,1)S(1)}, u32[]{:S(2)}) copy-start(pred[4]{0:T(512)(128)(4,1)S(1)} %get-tuple-element.43) | copy-start | bytes 16
  418.5 67.7 %copy-start.14 = (pred[4]{0:T(512)(128)(4,1)}, pred[4]{0:T(512)(128)(4,1)S(1)}, u32[]{:S(2)}) copy-start(pred[4]{0:T(512)(128)(4,1)S(1)} %get-tuple-element.44) | copy-start | bytes 16
  489.0 35.6 %copy-start.3 = (bf16[192,720]{1,0:T(8,128)(2,1)S(1)}, bf16[192,720]{1,0:T(8,128)(2,1)}, u32[]{:S(2)}) copy-start(bf16[192,720]{1,0:T(8,128)(2,1)} %fusion.63) | copy-start | bytes 829444
  489.0 35.6 %copy-start.4 = (bf16[192,720]{1,0:T(8,128)(2,1)S(1)}, bf16[192,720]{1,0:T(8,128)(2,1)}, u32[]{:S(2)}) copy-start(bf16[192,720]{1,0:T(8,128)(2,1)} %fusion.62) | copy-start | bytes 829444
  491.6 37.1 %copy-start.11 = (f32[2880]{0:T(1024)S(1)}, f32[2880]{0:T(1024)}, u32[]{:S(2)}) copy-start(f32[2880]{0:T(1024)} %param.40) | copy-start | bytes 34564
  525.7 16.8 %copy-start.1 = (bf16[512,2880]{0,1:T(8,128)(2,1)S(1)}, bf16[512,2880]{0,1:T(8,128)(2,1)}, u32[]{:S(2)}) copy-start(bf16[512,2880]{0,1:T(8,128)(2,1)} %param.31) | copy-start | bytes 8847364
Sparse Core Ops, SparseCore 0:
  9.6 50.7 all-gather.6
  87.5 38.2 reduce-scatter.12
  129.0 29.5 all-gather.10
  174.5 38.9 reduce-scatter.14
  216.8 29.5 all-gather.8
  418.4 33.2 reduce-scatter.16
  491.7 31.0 reduce-scatter.18
where the time goes:
time: 559 us; the launch traced here: 550 us
  waiting for transfers between devices  338 us (60%)
  matrix products  97.5 us (17%)
  local copies, waits for them, and re-layouts  50.3 us (9%)
  starting transfers between devices  19.9 us (4%)
  other arithmetic  19.2 us (3%)
  between operations  15 us (3%)
  blocking collectives  9.24 us (2%)
    unnamed x11, waiting for transfers between devices  139 us
    all_to_all x2, waiting for transfers between devices, shards(): lax.all_to_all(shares_out, 'expert', split_axis=0, concat_axis=0, tiled=T...  66.1 us
    all_gather x1, waiting for transfers between devices, shards(): gathered_rows = lax.all_gather(hidden, 'dp', axis=1, tiled=True)  46.6 us
    all_gather x2, waiting for transfers between devices, shards(): column_h = lax.all_gather(resid_h, 'dp', axis=1, tiled=True)  45 us
    all_to_all x2, waiting for transfers between devices, shards(): lax.all_to_all(outgoing, 'expert', split_axis=0, concat_axis=0, tiled=True)  41.6 us
    dot_general x2, matrix products, shards(): jnp.dot(activated, down_weight, preferred_element_type=jnp.float32)  33.7 us
    dot_general x2, matrix products, shards(): up_part = jnp.dot(rows_in, up_weight, preferred_element_type=jnp.float32)  20.7 us
    unnamed x49, local copies, waits for them, and re-layouts  12.3 us
  transfers between devices with their start and end apart: 11, of which 10 were waited for; matrix products, arithmetic and copies ran while one was open for 18% of the time, Pallas kernels for 0%

commit v1 on v0

--- a/solution.py
+++ b/solution.py
@@ -98,7 +98,13 @@
     segment_row = segments[0]
     adapter_row = request_adapter[0]
     col_tokens = segment_row.shape[0]
-    gathered_rows = lax.all_gather(hidden, "dp", axis=1, tiled=True)
+    size = lax.axis_size("dp")
+    moving, tiles = (hidden, [hidden])
+    for _ in range(size - 1):
+        moving = lax.ppermute(moving, "dp", [(i, (i + 1) % size) for i in range(size)])
+        tiles.insert(0, moving)
+    line = jnp.concatenate(tiles, axis=1)
+    gathered_rows = jnp.roll(line, (lax.axis_index("dp") + 1) * hidden.shape[1], axis=1)
     width = gathered_rows.shape[1]
     normalized_hidden = rms_scale(gathered_rows.astype(jnp.float32), attention_gain).astype(
         jnp.bfloat16

time: 559 us -> 568 us (1.016)
  waiting for transfers between devices: 338 us -> 325 us
  local copies, waits for them, and re-layouts: 50.3 us -> 60.2 us
    all_gather x1 -> x0, waiting for transfers between devices: 46.6 us -> none  [shards(): gathered_rows = lax.all_gather(hidden, 'dp', axis=1, tiled=True)]
    ppermute x0 -> x3, waiting for transfers between devices: none -> 34.7 us  [shards(): lax.ppermute(moving, 'dp', [(i, (i + 1) % size) for i in range(size)])]
    unnamed x49 -> x74, local copies, waits for them, and re-layouts: 12.3 us -> 19.5 us
    unnamed x11 -> x10, waiting for transfers between devices: 139 us -> 138 us
  transfers between devices with their start and end apart: 11 -> 13, of which waited for: 10 -> 12; matrix products, arithmetic and copies ran while one was open for 18% -> 19% of each run, Pallas kernels for 0% -> 0%
where the time goes in v1:
time: 568 us; the launch traced here: 557 us
  waiting for transfers between devices  325 us (57%)
  matrix products  100 us (18%)
  local copies, waits for them, and re-layouts  60.2 us (11%)
  other arithmetic  24.6 us (4%)
  starting transfers between devices  22.9 us (4%)
  between operations  15.2 us (3%)
  blocking collectives  9.22 us (2%)
    unnamed x10, waiting for transfers between devices  138 us
    all_to_all x2, waiting for transfers between devices, shards(): lax.all_to_all(shares_out, 'expert', split_axis=0, concat_axis=0, tiled=T...  66.1 us
    all_gather x2, waiting for transfers between devices, shards(): column_h = lax.all_gather(resid_h, 'dp', axis=1, tiled=True)  45.1 us
    all_to_all x2, waiting for transfers between devices, shards(): lax.all_to_all(outgoing, 'expert', split_axis=0, concat_axis=0, tiled=True)  41.6 us
    ppermute x3, waiting for transfers between devices, shards(): lax.ppermute(moving, 'dp', [(i, (i + 1) % size) for i in range(size)])  34.7 us
    dot_general x2, matrix products, shards(): jnp.dot(activated, down_weight, preferred_element_type=jnp.float32)  33.7 us
    dot_general x2, matrix products, shards(): up_part = jnp.dot(rows_in, up_weight, preferred_element_type=jnp.float32)  20.7 us
    unnamed x74, local copies, waits for them, and re-layouts  19.5 us
  transfers between devices with their start and end apart: 13, of which 12 were waited for; matrix products, arithmetic and copies ran while one was open for 19% of the time, Pallas kernels for 0%

profile of v1, /device:TPU:0, one launch (start us, length us, event | category | flops | bytes accessed | tf_op | source)
XLA Modules:
  0.0 557.3 jit_solution(14895301659038421166)
XLA Ops:
  7.2 3.1 collective-permute-start
  15.8 9.4 %collective-permute-done = bf16[384,720]{0,1:T(8,128)(2,1)} collective-permute-done((bf16[384,720]{0,1:T(8,128)(2,1)}, bf16[384,720]{0,1:T(8,128)(2,1)}, u32[]{:S(2)}, u32[]{:S(2)}) %collective-permute-start) | collective-permute-done | bytes 552992 | tf_op jit(solution)/shard_map/ppermute | solution.py:104
  28.1 12.8 %collective-permute-done.1 = bf16[384,720]{0,1:T(8,128)(2,1)S(1)} collective-permute-done((bf16[384,720]{0,1:T(8,128)(2,1)}, bf16[384,720]{0,1:T(8,128)(2,1)S(1)}, u32[]{:S(2)}, u32[]{:S(2)}) %collective-permute-start.1) | collective-permute-done | bytes 552992 | tf_op jit(solution)/shard_map/ppermute | solution.py:104
  43.1 12.4 %collective-permute-done.2 = bf16[384,720]{0,1:T(8,128)(2,1)S(1)} collective-permute-done((bf16[384,720]{0,1:T(8,128)(2,1)S(1)}, bf16[384,720]{0,1:T(8,128)(2,1)S(1)}, u32[]{:S(2)}, u32[]{:S(2)}) %collective-permute-start.2) | collective-permute-done | bytes 552992 | tf_op jit(solution)/shard_map/ppermute | solution.py:104
  58.4 2.0 copy-done.5
  61.7 4.7 convolution_multiply_fusion
  66.4 6.2 %fusion.56 = f32[384,640]{1,0:T(8,128)} fusion(f32[384,640]{1,0:T(8,128)} %convolution_multiply_fusion, bf16[2880,1,640]{2,0,1:T(8,128)(2,1)} %param.29, f32[2880]{0:T(1024)} %param.28, f32[384]{0:T(512)} %add_rsqrt_fusion, bf16[384,5760]{0,1:T(8,128)(2,1)} %copy-done.5, s32[]{:T(128)S(6)} %select_n.116), kind=kOutput, calls=%fused_computation.65 | convolution fusion | flops 1420247040 | bytes 7878660 | tf_op jit(solution)/shard_map/dot_general | solution.py:112
  72.6 2.5 copy.64
  79.1 2.2 fusion.19
  81.4 2.3 fusion.61
  87.0 2.7 convolution_convert_fusion.4
  90.1 2.9 fusion.141
  94.0 36.3 %reduce-scatter.13.cloned.1.call-done = bf16[896,192]{1,0:T(8,128)(2,1)} async-done(((bf16[3584,192]{1,0:T(8,128)(2,1)}), bf16[896,192]{1,0:T(8,128)(2,1)}) %reduce-scatter.13.cloned.1.call-update) | async-done | bytes 344080
  137.2 3.4 scatter_custom_fusion.1
  140.6 22.6 %all-gather.8.cloned.1.call-done = bf16[4,720,192]{1,2,0:T(8,128)(2,1)} async-done(((bf16[1,720,192]{1,2,0:T(8,128)(2,1)}), bf16[4,720,192]{1,2,0:T(8,128)(2,1)}) %all-gather.8.cloned.1.call-update) | async-done | bytes 1105936 | tf_op jit(solution)/shard_map/all_gather | solution.py:209
  163.2 2.2 copy.75
  167.0 4.4 convolution_convert_fusion.1
  171.5 4.7 all-to-all-start
  177.2 41.2 %reduce-scatter.15.cloned.1.call-done = bf16[896,192]{1,0:T(8,128)(2,1)} async-done(((bf16[3584,192]{1,0:T(8,128)(2,1)}), bf16[896,192]{1,0:T(8,128)(2,1)}) %reduce-scatter.15.cloned.1.call-update) | async-done | bytes 344080
  225.2 3.6 scatter_custom_fusion
  228.8 22.4 %all-gather.6.cloned.1.call-done = bf16[4,720,192]{1,2,0:T(8,128)(2,1)} async-done(((bf16[1,720,192]{1,2,0:T(8,128)(2,1)}), bf16[4,720,192]{1,2,0:T(8,128)(2,1)}) %all-gather.6.cloned.1.call-update) | async-done | bytes 1105936 | tf_op jit(solution)/shard_map/all_gather | solution.py:209
  251.2 3.2 copy.72
  254.4 2.7 reshape.552
  257.8 4.4 convolution_convert_fusion
  262.2 4.7 all-to-all-start.1
  266.9 10.4 %fusion.4 = f32[1024,720]{0,1:T(8,128)} fusion(bf16[1024,2944]{1,0:T(8,128)(2,1)} %bitcast.45, bf16[1,2880,720]{1,2,0:T(8,128)(2,1)} %param.38), kind=kOutput, calls=%fused_computation.16 | convolution fusion | flops 4246732800 | bytes 13125632 | tf_op jit(solution)/shard_map/dot_general | solution.py:240
  277.3 16.8 %convolution_convert_fusion.2 = bf16[1024,2944]{1,0:T(8,128)(2,1)} fusion(bf16[720,2880]{1,0:T(8,128)(2,1)} %bitcast.185, f32[1024,720]{0,1:T(8,128)} %fusion.4, bf16[1,2880,720]{1,2,0:T(8,128)(2,1)} %param.37, bf16[1024,2944]{1,0:T(8,128)(2,1)} %bitcast.45), kind=kOutput, calls=%fused_computation.12 | convolution fusion | flops 8596750336 | bytes 23302144 | tf_op jit(solution)/shard_map/dot_general | solution.py:245
  294.1 41.6 %all-to-all-done.1 = bf16[8,128,2944]{2,1,0:T(8,128)(2,1)} async-done(((bf16[8,128,2944]{2,1,0:T(8,128)(2,1)}), bf16[8,128,2944]{2,1,0:T(8,128)(2,1)}, u32[]{:S(2)}, u32[]{:S(2)}) %all-to-all-start.1) | async-done | bytes 6029344 | tf_op jit(solution)/shard_map/all_to_all | solution.py:233
  335.7 4.9 all-to-all-start.3
  340.7 10.4 %fusion.8 = f32[1024,720]{0,1:T(8,128)} fusion(bf16[1024,2944]{1,0:T(8,128)(2,1)} %bitcast.40, bf16[1,2880,720]{1,2,0:T(8,128)(2,1)} %param.38), kind=kOutput, calls=%fused_computation.20 | convolution fusion | flops 4246732800 | bytes 13125632 | tf_op jit(solution)/shard_map/dot_general | solution.py:240
  351.1 16.8 %convolution_convert_fusion.3 = bf16[1024,2944]{1,0:T(8,128)(2,1)} fusion(bf16[720,2880]{1,0:T(8,128)(2,1)} %bitcast.186, f32[1024,720]{0,1:T(8,128)} %fusion.8, bf16[1,2880,720]{1,2,0:T(8,128)(2,1)} %param.37, bf16[1024,2944]{1,0:T(8,128)(2,1)} %bitcast.40), kind=kOutput, calls=%fused_computation.13 | convolution fusion | flops 8596750336 | bytes 23302144 | tf_op jit(solution)/shard_map/dot_general | solution.py:245
  367.9 41.6 %all-to-all-done.3 = bf16[8,128,2944]{2,1,0:T(8,128)(2,1)} async-done(((bf16[8,128,2944]{2,1,0:T(8,128)(2,1)}), bf16[8,128,2944]{2,1,0:T(8,128)(2,1)}, u32[]{:S(2)}, u32[]{:S(2)}) %all-to-all-start.3) | async-done | bytes 6029344 | tf_op jit(solution)/shard_map/all_to_all | solution.py:249
  409.5 4.7 all-to-all-start.2
  414.8 5.8 %fusion.145 = (bf16[192,2880]{1,0:T(8,128)(2,1)}, f32[192,2880]{1,0:T(8,128)}) fusion(bf16[192,1024]{1,0:T(8,128)(2,1)S(1)} %fusion.51, bf16[1024,2944]{1,0:T(8,128)(2,1)} %bitcast.47), kind=kOutput, calls=%fused_computation.228 | convolution fusion | flops 1133015040 | bytes 9740288 | tf_op jit(solution)/shard_map/dot_general | solution.py:263
  420.6 2.5 copy.88
  423.9 2.2 gather_fusion
  426.1 30.4 %reduce-scatter.17.cloned.1.call-done = bf16[720,192]{1,0:T(8,128)(2,1)} async-done(((bf16[2880,192]{1,0:T(8,128)(2,1)}), bf16[720,192]{1,0:T(8,128)(2,1)}) %reduce-scatter.17.cloned.1.call-update) | async-done | bytes 276496
  456.6 1.8 copy.89
  458.4 24.6 %all-to-all-done.2 = bf16[8,128,2944]{2,1,0:T(8,128)(2,1)} async-done(((bf16[8,128,2944]{2,1,0:T(8,128)(2,1)}), bf16[8,128,2944]{2,1,0:T(8,128)(2,1)}, u32[]{:S(2)}, u32[]{:S(2)}) %all-to-all-start.2) | async-done | bytes 6029344 | tf_op jit(solution)/shard_map/all_to_all | solution.py:249
  483.0 5.8 %fusion.146 = (bf16[192,2880]{1,0:T(8,128)(2,1)}, f32[192,2880]{1,0:T(8,128)}) fusion(bf16[192,1024]{1,0:T(8,128)(2,1)S(1)} %fusion.50, bf16[1024,2944]{1,0:T(8,128)(2,1)} %bitcast.48), kind=kOutput, calls=%fused_computation.229 | convolution fusion | flops 1133015040 | bytes 9740288 | tf_op jit(solution)/shard_map/dot_general | solution.py:263
  488.8 2.2 gather_fusion.1
  491.5 2.4 pad_maximum_fusion.1
  493.9 2.5 copy.90
  498.8 28.9 %reduce-scatter.19.cloned.1.call-done = bf16[720,208]{1,0:T(8,128)(2,1)} async-done(((bf16[2880,208]{1,0:T(8,128)(2,1)}), bf16[720,208]{1,0:T(8,128)(2,1)}) %reduce-scatter.19.cloned.1.call-update) | async-done | bytes 299536
  530.2 2.2 add_convert_fusion
  532.4 2.1 copy.80
  536.4 9.2 %all-gather.2 = bf16[8,4,2880]{2,1,0:T(4,128)(2,1)S(1)} all-gather(bf16[1,4,2880]{2,1,0:T(4,128)(2,1)S(1)} %fusion.110), channel_id=1, replica_groups=mesh['dp'=4,'expert'=8] {'expert'}, dimensions={0}, use_global_device_ids=true | all-gather | bytes 207360 | tf_op jit(solution)/shard_map/all_gather | solution.py:292
  545.7 4.4 fusion.147
  (178 shorter events, 48.7 us)
Async XLA Ops:
  7.2 79.8 %copy-start = (bf16[512,2880]{0,1:T(8,128)(2,1)S(1)}, bf16[512,2880]{0,1:T(8,128)(2,1)}, u32[]{:S(2)}) copy-start(bf16[512,2880]{0,1:T(8,128)(2,1)} %param.31) | copy-start | bytes 8847364
  7.2 49.7 %copy-start.2 = (bf16[384,720]{0,1:T(8,128)(2,1)S(1)}, bf16[384,720]{0,1:T(8,128)(2,1)}, u32[]{:S(2)}) copy-start(bf16[384,720]{0,1:T(8,128)(2,1)} %param.23) | copy-start | bytes 1658884
  7.2 123.1 %reduce-scatter.13.cloned.1.call-start = ((), (), s32[]{:S(2)}) async-start(), calls=%async_computation.10 | async-start | bytes 2293760
  7.2 18.0 %collective-permute-start = (bf16[384,720]{0,1:T(8,128)(2,1)}, bf16[384,720]{0,1:T(8,128)(2,1)}, u32[]{:S(2)}, u32[]{:S(2)}) collective-permute-start(bf16[384,720]{0,1:T(8,128)(2,1)} %param.23), channel_id=1, source_target_pairs={{0,8},{8,16},{16,24},{24,0},{1,9},{9,17},{17,25},{25,1},{2,10},{10... | collective-permute-start | bytes 1658888 | tf_op jit(solution)/shard_map/ppermute | solution.py:104
  13.5 1.4 copy-start.17
  15.8 25.2 %copy-start.12 = (bf16[384,48]{0,1:T(8,128)(2,1)}, bf16[384,48]{0,1:T(8,128)(2,1)S(1)}, u32[]{:S(2)}) copy-start(bf16[384,48]{0,1:T(8,128)(2,1)S(1)} %dynamic_update_slice.5) | copy-start | bytes 110596
  25.2 15.7 %collective-permute-start.1 = (bf16[384,720]{0,1:T(8,128)(2,1)}, bf16[384,720]{0,1:T(8,128)(2,1)S(1)}, u32[]{:S(2)}, u32[]{:S(2)}) collective-permute-start(bf16[384,720]{0,1:T(8,128)(2,1)} %collective-permute-done), channel_id=1, source_target_pairs={{0,8},{8,16},{16,24},{24,0},{1,9},{9,17},{17,25},{25,1},{2,10},{10... | collective-permute-start | bytes 1658888 | tf_op jit(solution)/shard_map/ppermute | solution.py:104
  25.2 17.9 %copy-start.23 = (f32[32]{0:T(128)}, f32[32]{0:T(128)S(1)}, u32[]{:S(2)}) copy-start(f32[32]{0:T(128)S(1)} %multiply_power_fusion) | copy-start | bytes 388
  28.1 15.0 %copy-start.16 = (f32[384]{0:T(512)}, f32[384]{0:T(512)S(1)}, u32[]{:S(2)}) copy-start(f32[384]{0:T(512)S(1)} %fusion.119) | copy-start | bytes 4612
  40.9 14.6 %collective-permute-start.2 = (bf16[384,720]{0,1:T(8,128)(2,1)S(1)}, bf16[384,720]{0,1:T(8,128)(2,1)S(1)}, u32[]{:S(2)}, u32[]{:S(2)}) collective-permute-start(bf16[384,720]{0,1:T(8,128)(2,1)S(1)} %collective-permute-done.1), channel_id=1, source_target_pairs={{0,8},{8,16},{16,24},{24,0},{1,9},{9,17},{17,25},{25,1},{2,10},{10... | collective-permute-start | bytes 1658888 | tf_op jit(solution)/shard_map/ppermute | solution.py:104
  58.4 2.0 copy-start.5
  78.1 3.2 copy-start.25
  78.1 3.3 copy-start.11
  81.4 3.0 copy-start.14
  83.6 0.8 copy-start.9
  87.0 2.7 copy-start.13
  87.0 2.8 copy-start.10
  93.0 0.9 copy-start.19
  93.0 0.9 copy-start.24
  93.0 39.4 %copy-start.7 = (bf16[128,720]{0,1:T(8,128)(2,1)S(1)}, bf16[128,720]{0,1:T(8,128)(2,1)}, u32[]{:S(2)}) copy-start(bf16[128,720]{0,1:T(8,128)(2,1)} %param.35) | copy-start | bytes 552964
  93.0 70.2 %all-gather.8.cloned.1.call-start = ((), (), s32[]{:S(2)}) async-start(), calls=%async_computation.9 | async-start | bytes 1474560 | tf_op jit(solution)/shard_map/all_gather | solution.py:209
  133.4 33.3 %copy-start.15 = (f32[2880]{0:T(1024)S(1)}, f32[2880]{0:T(1024)}, u32[]{:S(2)}) copy-start(f32[2880]{0:T(1024)} %param.36) | copy-start | bytes 34564
  171.5 85.7 %all-to-all-start = ((bf16[8,128,2944]{2,1,0:T(8,128)(2,1)}), bf16[8,128,2944]{2,1,0:T(8,128)(2,1)}, u32[]{:S(2)}, u32[]{:S(2)}) async-start(bf16[8,128,2944]{2,1,0:T(8,128)(2,1)} %bitcast.151), calls=%async_computation | async-start | bytes 12058624 | tf_op jit(solution)/shard_map/all_to_all | solution.py:233
  176.2 44.3 %copy-start.8 = (bf16[128,720]{0,1:T(8,128)(2,1)S(1)}, bf16[128,720]{0,1:T(8,128)(2,1)}, u32[]{:S(2)}) copy-start(bf16[128,720]{0,1:T(8,128)(2,1)} %param.35) | copy-start | bytes 552964
  176.2 42.1 %reduce-scatter.15.cloned.1.call-start = ((), (), s32[]{:S(2)}) async-start(), calls=%async_computation.11 | async-start | bytes 2293760
  176.9 74.3 %all-gather.6.cloned.1.call-start = ((), (), s32[]{:S(2)}) async-start(), calls=%async_computation.8 | async-start | bytes 1474560 | tf_op jit(solution)/shard_map/all_gather | solution.py:209
  262.2 73.5 %all-to-all-start.1 = ((bf16[8,128,2944]{2,1,0:T(8,128)(2,1)}), bf16[8,128,2944]{2,1,0:T(8,128)(2,1)}, u32[]{:S(2)}, u32[]{:S(2)}) async-start(bf16[8,128,2944]{2,1,0:T(8,128)(2,1)} %bitcast.152), calls=%async_computation.1 | async-start | bytes 12058624 | tf_op jit(solution)/shard_map/all_to_all | solution.py:233
  335.7 73.7 %all-to-all-start.3 = ((bf16[8,128,2944]{2,1,0:T(8,128)(2,1)}), bf16[8,128,2944]{2,1,0:T(8,128)(2,1)}, u32[]{:S(2)}, u32[]{:S(2)}) async-start(bf16[8,128,2944]{2,1,0:T(8,128)(2,1)} %bitcast.160), calls=%async_computation.3 | async-start | bytes 12058624 | tf_op jit(solution)/shard_map/all_to_all | solution.py:249
  409.5 73.5 %all-to-all-start.2 = ((bf16[8,128,2944]{2,1,0:T(8,128)(2,1)}), bf16[8,128,2944]{2,1,0:T(8,128)(2,1)}, u32[]{:S(2)}, u32[]{:S(2)}) async-start(bf16[8,128,2944]{2,1,0:T(8,128)(2,1)} %bitcast.159), calls=%async_computation.2 | async-start | bytes 12058624 | tf_op jit(solution)/shard_map/all_to_all | solution.py:249
  414.2 42.4 %reduce-scatter.17.cloned.1.call-start = ((), (), s32[]{:S(2)}) async-start(), calls=%async_computation.12 | async-start | bytes 1843200
  423.2 104.5 %reduce-scatter.19.cloned.1.call-start = ((), (), s32[]{:S(2)}) async-start(), calls=%async_computation.13 | async-start | bytes 1843200
  423.3 67.7 %copy-start.20 = (pred[4]{0:T(512)(128)(4,1)}, pred[4]{0:T(512)(128)(4,1)S(1)}, u32[]{:S(2)}) copy-start(pred[4]{0:T(512)(128)(4,1)S(1)} %get-tuple-element.42) | copy-start | bytes 16
  423.4 67.7 %copy-start.21 = (pred[4]{0:T(512)(128)(4,1)}, pred[4]{0:T(512)(128)(4,1)S(1)}, u32[]{:S(2)}) copy-start(pred[4]{0:T(512)(128)(4,1)S(1)} %get-tuple-element.43) | copy-start | bytes 16
  423.4 67.7 %copy-start.22 = (pred[4]{0:T(512)(128)(4,1)}, pred[4]{0:T(512)(128)(4,1)S(1)}, u32[]{:S(2)}) copy-start(pred[4]{0:T(512)(128)(4,1)S(1)} %get-tuple-element.44) | copy-start | bytes 16
  491.5 38.7 %copy-start.3 = (bf16[192,720]{1,0:T(8,128)(2,1)S(1)}, bf16[192,720]{1,0:T(8,128)(2,1)}, u32[]{:S(2)}) copy-start(bf16[192,720]{1,0:T(8,128)(2,1)} %fusion.65) | copy-start | bytes 829444
  491.5 38.7 %copy-start.4 = (bf16[192,720]{1,0:T(8,128)(2,1)S(1)}, bf16[192,720]{1,0:T(8,128)(2,1)}, u32[]{:S(2)}) copy-start(bf16[192,720]{1,0:T(8,128)(2,1)} %fusion.64) | copy-start | bytes 829444
  493.9 42.4 %copy-start.18 = (f32[2880]{0:T(1024)S(1)}, f32[2880]{0:T(1024)}, u32[]{:S(2)}) copy-start(f32[2880]{0:T(1024)} %param.40) | copy-start | bytes 34564
  528.8 0.7 copy-start.6
  530.2 19.9 %copy-start.1 = (bf16[512,2880]{0,1:T(8,128)(2,1)S(1)}, bf16[512,2880]{0,1:T(8,128)(2,1)}, u32[]{:S(2)}) copy-start(bf16[512,2880]{0,1:T(8,128)(2,1)} %param.31) | copy-start | bytes 8847364
Sparse Core Ops, SparseCore 0:
  93.1 37.1 reduce-scatter.12
  133.6 29.5 all-gather.7
  179.3 38.9 reduce-scatter.14
  221.6 29.5 all-gather.5
  423.3 33.2 reduce-scatter.16
  496.6 31.0 reduce-scatter.18
